TPU v7x, 256 devices: a whole 4x4x8 slice. The times are simulated.
256 devices in a mesh: sample: 16 (over y_hi, z), space: 16 (over y_lo, x, core).
Axes of the slice: x: 4, y: 4 (y_hi: 2, y_lo: 2; y = y_hi * 2 + y_lo), z: 8, core: 2. Of those that a mesh axis runs over, the one named last changes fastest.
Arguments:
- volumes: bfloat16 [16, 32, 64, 1024], P('sample', None, 'space'), may hold values from -6 to 6
- first_weight: bfloat16 [64, 864], replicated, may hold values from -0.21875 to 0.21875
- first_bias: float32 [64], replicated, may hold values from -3 to 3
- second_weight: bfloat16 [128, 1728], replicated, may hold values from -0.15625 to 0.15625
- second_bias: float32 [128], replicated, may hold values from -3 to 3
- cotangent: bfloat16 [16, 128, 32, 256], P('sample', None, 'space'), may hold values from -6 to 6
Outputs:
- activation: bfloat16 [16, 128, 32, 256], P('sample', None, 'space')
- input_grad: bfloat16 [16, 32, 64, 1024], P('sample', None, 'space')
- first_wgrad: float32 [64, 864], replicated
- first_bgrad: float32 [64], replicated
- second_wgrad: float32 [128, 1728], replicated
- second_bgrad: float32 [128], replicated
All inputs are finite; a program needn't handle non-finite values.
Results may differ from a plain program's by a relative error of at most 0.013.
Values may be sent and summed in bfloat16 or wider, within the bound.
No kernel may reach another device: no remote copies, remote signals or barrier semaphores. Data moves between devices by JAX's collectives and lax.ppermute only.
A program may use at most 64 MiB of HBM per device.

v0:
```python
import math

import jax
import jax.numpy as jnp
from jax import lax
from jax.sharding import PartitionSpec as P

CH_IN = 32
CH_MID = 64
CH_OUT = 128
VOL_HEIGHT = 64
VOL_WIDTH = 16


LAYOUT_SPEC = ("NCDHW", "OIDHW", "NCDHW")


def padded_2(x, sides, width):
    for axis, dim in sides:
        size, length = (lax.axis_size(axis), x.shape[dim])
        up = [(i, (i + 1) % size) for i in range(size - 1)]
        down = [(j, i) for i, j in up]
        last = lax.slice_in_dim(x, length - width, length, axis=dim)
        initial = lax.slice_in_dim(x, 0, width, axis=dim)
        before = lax.ppermute(last, axis, up)
        after = lax.ppermute(initial, axis, down)
        x = jnp.concatenate([before, x, after], axis=dim)
    return x


def from_partner(block, axis, stride):
    count = lax.axis_size(axis)
    route = []
    for low in range(count):
        high = low | 1 << stride
        if high != low and high < count:
            route += [(low, high), (high, low)]
    return lax.ppermute(block, axis, route)


def shifted(x, axis, by):
    size = lax.axis_size(axis)
    pairs = [(i, i + by) for i in range(size) if 0 <= i + by < size]
    return lax.ppermute(x, axis, pairs)


def as_sent(x):

    def short(part):
        return part.astype(jnp.bfloat16) if part.dtype == jnp.float32 else part

    return jax.tree.map(short, x)


def kernel_of(weight, channels):
    return weight.reshape(weight.shape[0], 3, 3, 3, channels).transpose(0, 4, 1, 2, 3)


def flipped(kernel):
    return jnp.flip(kernel, (2, 3, 4)).transpose(1, 0, 2, 3, 4)


def correlate(padded, kernel):
    return lax.conv_general_dilated(
        padded,
        kernel,
        (1, 1, 1),
        "VALID",
        dimension_numbers=LAYOUT_SPEC,
        preferred_element_type=jnp.float32,
    )


def pad_sides(volume, depth_pad, height_pad):
    return jnp.pad(
        volume, ((0, 0), (0, 0), (depth_pad, depth_pad), (height_pad, height_pad), (1, 1))
    )


def silu_slope(values_in):
    sigmoid_v = jax.nn.sigmoid(values_in)
    return sigmoid_v * (1.0 + values_in * (1.0 - sigmoid_v))


def upsampled(pooled_grad, slope):
    sample_count, channels, planes, rows_half, cols_half = pooled_grad.shape
    shaped = slope.reshape(sample_count, channels, planes, 2, rows_half, 2, cols_half, 2)
    return (pooled_grad[:, :, :, None, :, None, :, None] * 0.125 * shaped).reshape(slope.shape)


def weight_grad(padded, slope_grad):
    depth_cells, height_cells, width_cells = slope_grad.shape[2:]
    columns = []
    for offset in range(27):
        depth_off, height_off, width_off = (offset // 9, offset // 3 % 3, offset % 3)
        window = padded[
            :,
            :,
            depth_off : depth_off + depth_cells,
            height_off : height_off + height_cells,
            width_off : width_off + width_cells,
        ]
        columns.append(
            lax.dot_general(
                slope_grad,
                window,
                (((0, 2, 3, 4), (0, 2, 3, 4)), ((), ())),
                preferred_element_type=jnp.float32,
            )
        )
    return jnp.concatenate(columns, axis=1)


def butterfly(pieces_all, mover, own_index, bit_levels):
    for bit_level in range(bit_levels):
        step_size = 1 << bit_level
        outer_count = pieces_all.shape[0] // (2 * step_size)
        trailing = pieces_all.shape[1:]
        grouped = pieces_all.reshape((outer_count, 2, step_size) + trailing)
        lower_half = grouped[:, 0]
        upper_half = grouped[:, 1]
        bit_set = own_index >> bit_level & 1 == 1
        kept_half = jnp.where(bit_set, upper_half, lower_half)
        sent_half = jnp.where(bit_set, lower_half, upper_half)
        arrived = mover(sent_half, bit_level)
        new_lower = jnp.where(bit_set, arrived, kept_half)
        new_upper = jnp.where(bit_set, kept_half, arrived)
        pieces_all = jnp.stack([new_lower, new_upper], axis=1).reshape(pieces_all.shape)
    return pieces_all


def slabs_to_blocks(slab, mover, own_index, block_side, bit_levels):
    sample_count, channels, planes, rows_all, row_cells = slab.shape
    rows_block = rows_all // block_side
    pieces_all = jnp.moveaxis(
        slab.reshape(sample_count, channels, planes, block_side, rows_block * row_cells), 3, 0
    )
    arrived = jnp.moveaxis(butterfly(pieces_all, mover, own_index, bit_levels), 0, 2)
    return arrived.reshape(sample_count, channels, block_side * planes, rows_block, row_cells)


def blocks_to_slabs(block, mover, own_index, block_side, bit_levels):
    sample_count, channels, planes_all, rows_block, row_cells = block.shape
    planes = planes_all // block_side
    pieces_all = jnp.moveaxis(
        block.reshape(sample_count, channels, block_side, planes, rows_block * row_cells), 2, 0
    )
    arrived = jnp.moveaxis(butterfly(pieces_all, mover, own_index, bit_levels), 0, 3)
    return arrived.reshape(sample_count, channels, planes, block_side * rows_block * row_cells)


def block_halo(block, movers, own_index, block_side):
    sample_count, channels, planes, rows_block, row_cells = block.shape
    block_column = own_index % block_side
    last_row = block[:, :, :, rows_block - 1].reshape(sample_count, channels, planes * row_cells)
    first_row = block[:, :, :, 0].reshape(sample_count, channels, planes * row_cells)
    last_row = jnp.where(block_column == block_side - 1, jnp.zeros_like(last_row), last_row)
    first_row = jnp.where(block_column == 0, jnp.zeros_like(first_row), first_row)
    from_prev = movers[0](last_row)
    from_next = movers[1](first_row)
    tall_block = jnp.concatenate(
        [
            from_prev.reshape(sample_count, channels, planes, 1, row_cells),
            block,
            from_next.reshape(sample_count, channels, planes, 1, row_cells),
        ],
        axis=3,
    )
    top_plane = tall_block[:, :, planes - 1].reshape(
        sample_count, channels, (rows_block + 2) * row_cells
    )
    bottom_plane = tall_block[:, :, 0].reshape(sample_count, channels, (rows_block + 2) * row_cells)
    from_below = movers[2](top_plane)
    from_above = movers[3](bottom_plane)
    full_block = jnp.concatenate(
        [
            from_below.reshape(sample_count, channels, 1, rows_block + 2, row_cells),
            tall_block,
            from_above.reshape(sample_count, channels, 1, rows_block + 2, row_cells),
        ],
        axis=2,
    )
    return jnp.pad(full_block, ((0, 0), (0, 0), (0, 0), (0, 0), (1, 1)))


def per_device(volumes, first_weight, first_bias, second_weight, second_bias, cotangent):
    sample_count = volumes.shape[0]
    depth_cells = volumes.shape[2]
    plane_cells = volumes.shape[3]
    space_count = lax.axis_size("space")
    total_samples = sample_count * lax.axis_size("sample")
    half_height = VOL_HEIGHT // 2
    half_width = VOL_WIDTH // 2
    pooled_planes = depth_cells // 2
    grad_scale = 1.0 / math.sqrt(
        total_samples * depth_cells * space_count * VOL_HEIGHT * VOL_WIDTH / 8.0
    )
    kernel_one = kernel_of(first_weight, CH_IN)
    kernel_two = kernel_of(second_weight, CH_MID)
    haloed_in = padded_2(volumes, (("space", 2),), 1)
    padded_in = pad_sides(
        haloed_in.reshape(sample_count, CH_IN, depth_cells + 2, VOL_HEIGHT, VOL_WIDTH), 0, 1
    )
    first_pre = correlate(padded_in, kernel_one) + first_bias.reshape(1, CH_MID, 1, 1, 1)
    pooled = (
        jax.nn.silu(first_pre)
        .reshape(sample_count, CH_MID, pooled_planes, 2, half_height, 2, half_width, 2)
        .mean(axis=(3, 5, 7))
        .astype(jnp.bfloat16)
    )
    cot_cells = cotangent.reshape(sample_count, CH_OUT, pooled_planes, half_height, half_width)
    own_index = lax.axis_index("space")
    block_side = math.isqrt(space_count)
    bit_levels = block_side.bit_length() - 1
    pooled_block = slabs_to_blocks(
        pooled,
        lambda piece_in, bit_level: from_partner(piece_in, "space", bit_level),
        own_index,
        block_side,
        bit_levels,
    )
    cot_block = slabs_to_blocks(
        cot_cells,
        lambda piece_in, bit_level: from_partner(piece_in, "space", bit_level),
        own_index,
        block_side,
        bit_levels,
    )
    pooled_movers = (
        lambda piece_in: shifted(piece_in, "space", 1),
        lambda piece_in: shifted(piece_in, "space", -1),
        lambda piece_in: shifted(piece_in, "space", block_side),
        lambda piece_in: shifted(piece_in, "space", -block_side),
    )
    padded_pool = block_halo(pooled_block, pooled_movers, own_index, block_side)
    second_pre = correlate(padded_pool, kernel_two) + second_bias.reshape(1, CH_OUT, 1, 1, 1)
    second_grad = (cot_block.astype(jnp.float32) * silu_slope(second_pre)).astype(jnp.bfloat16)
    grad_movers = (
        lambda piece_in: shifted(piece_in, "space", 1),
        lambda piece_in: shifted(piece_in, "space", -1),
        lambda piece_in: shifted(piece_in, "space", block_side),
        lambda piece_in: shifted(piece_in, "space", -block_side),
    )
    padded_grad = block_halo(second_grad, grad_movers, own_index, block_side)
    grad_block = correlate(padded_grad, flipped(kernel_two))
    activation = blocks_to_slabs(
        jax.nn.silu(second_pre).astype(jnp.bfloat16),
        lambda piece_in, bit_level: from_partner(piece_in, "space", bit_level),
        own_index,
        block_side,
        bit_levels,
    )
    pooled_grad = blocks_to_slabs(
        grad_block,
        lambda piece_in, bit_level: from_partner(as_sent(piece_in), "space", bit_level).astype(
            piece_in.dtype
        ),
        own_index,
        block_side,
        bit_levels,
    )
    second_wgrad = weight_grad(padded_pool, second_grad)
    second_bgrad = jnp.sum(second_grad, axis=(0, 2, 3, 4), dtype=jnp.float32)
    pooled_cells = pooled_grad.reshape(sample_count, CH_MID, pooled_planes, half_height, half_width)
    first_grad = upsampled(pooled_cells, silu_slope(first_pre)).astype(jnp.bfloat16)
    first_wgrad = weight_grad(padded_in, first_grad)
    first_bgrad = jnp.sum(first_grad, axis=(0, 2, 3, 4), dtype=jnp.float32)
    first_wgrad, first_bgrad, second_wgrad, second_bgrad = lax.psum(
        (first_wgrad, first_bgrad, second_wgrad, second_bgrad), ("sample", "space")
    )
    flip_one = flipped(kernel_one)
    haloed_grad = padded_2(
        first_grad.reshape(sample_count, CH_MID, depth_cells, plane_cells), (("space", 2),), 1
    )
    input_sum = correlate(
        pad_sides(
            haloed_grad.reshape(sample_count, CH_MID, depth_cells + 2, VOL_HEIGHT, VOL_WIDTH), 0, 1
        ),
        flip_one,
    )
    input_sum = input_sum.reshape(sample_count, CH_IN, depth_cells, plane_cells)
    input_grad = input_sum.astype(jnp.bfloat16)
    return (
        activation,
        input_grad,
        first_wgrad * grad_scale,
        first_bgrad * grad_scale,
        second_wgrad * grad_scale,
        second_bgrad * grad_scale,
    )


def solution(mesh):
    in_specs = (
        P("sample", None, "space", None),
        P(),
        P(),
        P(),
        P(),
        P("sample", None, "space", None),
    )
    out_specs = (
        P("sample", None, "space", None),
        P("sample", None, "space", None),
        P(),
        P(),
        P(),
        P(),
    )
    return jax.shard_map(
        per_device, mesh=mesh, in_specs=in_specs, out_specs=out_specs, check_vma=False
    )
```

profile of v0, /device:TPU:1, one launch (start us, length us, event | category | flops | bytes accessed | tf_op | source)
XLA Modules:
  0.0 507.5 jit_solution(7699567085457309473)
XLA Ops:
  7.2 1.3 fusion.266
  8.5 4.5 collective-permute-start
  13.0 1.9 collective-permute-start.1
  16.2 1.1 copy.304
  17.3 2.1 collective-permute-done.1
  19.3 1.4 pad_maximum_fusion
  21.6 1.4 copy.485
  23.0 1.3 pad.14.clone
  24.3 3.9 copy.303
  28.2 2.0 slice.353
  30.3 6.5 %add_multiply_fusion = (f32[4,64,8,3,64]{4,2,3,1,0:T(8,128)}, f32[4,64,8,3,64]{4,2,3,1,0:T(8,128)S(1)}) fusion(f32[64]{0:T(128)S(1)} %copy-done.7, pred[8,3]{0,1:T(4,128)(4,1)S(1)} %copy-done.9, bf16[64,3,3,3,32]{0,4,3,2,1:T(8,128)(2,1)S(1)} %bitcast.906, bf16[32,6,64,1,7,2]{0,4,5,2,1,3:T(8,128)(2,1)S(1)} %slice.353, ...), kind=kOutput, calls=%fused_computation.16 | convolution fusion | flops 679280640 | bytes 4190488 | tf_op jit(solution)/shard_map/conv_general_dilated | solution.py:64
  37.4 1.5 slice.354
  38.9 2.9 reduce_sum.27
  42.2 1.2 collective-permute-done.2
  43.5 1.3 collective-permute-start.3
  45.3 1.3 copy.352
  46.6 2.4 copy.344
  49.1 1.5 slice.377
  50.8 2.6 collective-permute-start.5
  53.4 3.0 collective-permute-start.4
  57.8 1.3 collective-permute-start.7
  59.1 7.1 %collective-permute-start.6 = (bf16[1,64,80]{1,2,0:T(8,128)(2,1)S(1)}, bf16[1,64,80]{1,2,0:T(8,128)(2,1)S(1)}, u32[]{:S(2)}, u32[]{:S(2)}) collective-permute-start(bf16[1,64,80]{1,2,0:T(8,128)(2,1)S(1)} %bitcast.912), channel_id=1, source_target_pairs={{0,4},{1,5},{2,6},{3,7},{4,8},{5,9},{6,10},{7,11},{8,12},{9,13},{1... | collective-permute-start | bytes 30728 | tf_op jit(solution)/shard_map/ppermute | solution.py:44
  67.9 2.6 convert_reduce_fusion.1
  70.6 2.8 pad_maximum_fusion.4
  73.5 2.9 pad_slice_fusion.4
  76.3 2.9 pad_slice_fusion.5
  79.2 3.5 collective-permute-start.13
  82.7 2.9 collective-permute-start.12
  92.1 1.3 collective-permute-start.15
  93.4 8.2 %collective-permute-start.14 = (bf16[1,128,80]{1,2,0:T(8,128)(2,1)S(1)}, bf16[1,128,80]{1,2,0:T(8,128)(2,1)S(1)}, u32[]{:S(2)}, u32[]{:S(2)}) collective-permute-start(bf16[1,128,80]{1,2,0:T(8,128)(2,1)S(1)} %bitcast.913), channel_id=1, source_target_pairs={{0,4},{1,5},{2,6},{3,7},{4,8},{5,9},{6,10},{7,11},{8,12},{9,13},{1... | collective-permute-start | bytes 61448 | tf_op jit(solution)/shard_map/ppermute | solution.py:44
  102.8 2.8 fusion.123
  107.5 4.7 collective-permute-start.17
  112.8 1.5 collective-permute-done.17
  115.2 3.1 convert_reduce_fusion
  118.3 83.8 %all-reduce.2 = (f32[64]{0:T(128)S(1)}, f32[128]{0:T(128)S(1)}) all-reduce(f32[64]{0:T(128)S(1)} %get-tuple-element.43, f32[128]{0:T(128)S(1)} %get-tuple-element.40), channel_id=1, replica_groups=mesh['sample'=16,'space'=16] {'sample','space'}, use_global_device_ids=true, to_apply=%region_3.4 | all-reduce | flops 192 | bytes 1536 | tf_op jit(solution)/shard_map/psum | solution.py:268
  204.0 2.8 collective-permute-start.18
  206.8 2.6 collective-permute-start.19
  216.7 1.1 fusion.68
  217.7 1.1 fusion.67
  239.6 2.6 maximum_bitcast_fusion
  242.1 3.2 copy.486
  245.3 2.1 pad.16.clone
  247.4 2.8 copy.348
  250.3 2.0 slice.380
  252.4 11.1 %fusion.4 = bf16[4,64,8,3,32]{4,2,3,1,0:T(8,128)(2,1)S(1)} fusion(bf16[64,3,3,3,32]{0,4,3,2,1:T(8,128)(2,1)S(1)} %bitcast.907, bf16[64,6,64,1,7,2]{0,4,5,2,1,3:T(8,128)(2,1)S(1)} %slice.380, bf16[64,6,64,1,8,3]{0,4,5,2,1,3:T(8,128)(2,1)S(1)} %copy-done.2), kind=kOutput, calls=%fused_computation.6 | convolution fusion | flops 678297600 | bytes 2371584 | tf_op jit(solution)/shard_map/conv_general_dilated | solution.py:64
  265.7 1.2 copy.388
  266.9 229.5 %all-reduce.6.cloned.1.call-done = (f32[64,864]{0,1:T(8,128)}, f32[128,1728]{0,1:T(8,128)}) async-done(((f32[64,864]{0,1:T(8,128)}, f32[128,1728]{0,1:T(8,128)}), (f32[64,864]{0,1:T(8,128)}, f32[128,1728]{0,1:T(8,128)})) %all-reduce.6.cloned.1.call-update) | async-done | bytes 1105936 | tf_op jit(solution)/shard_map/psum | solution.py:268
  498.3 2.2 broadcast_multiply_fusion
  (168 shorter events, 51.8 us)
Async XLA Ops:
  7.2 60.7 %copy-start = (bf16[128,1728]{0,1:T(8,128)(2,1)S(1)}, bf16[128,1728]{0,1:T(8,128)(2,1)}, u32[]{:S(2)}) copy-start(bf16[128,1728]{0,1:T(8,128)(2,1)} %param.9) | copy-start | bytes 1327108
  7.2 489.2 %all-reduce.6.cloned.1.call-start = ((), (), s32[]{:S(2)}) async-start(), calls=%async_computation | async-start | bytes 2654208 | tf_op jit(solution)/shard_map/psum | solution.py:268
  8.5 8.7 %collective-permute-start = (bf16[1,32,1,1024]{3,2,1,0:T(2,128)(2,1)S(1)}, bf16[1,32,1,1024]{3,2,1,0:T(2,128)(2,1)S(1)}, u32[]{:S(2)}, u32[]{:S(2)}) collective-permute-start(bf16[1,32,1,1024]{3,2,1,0:T(2,128)(2,1)S(1)} %get-tuple-element.86), channel_id=1, source_target_pairs={{0,1},{1,2},{2,3},{3,4},{4,5},{5,6},{6,7},{7,8},{8,9},{9,10},{10,1... | collective-permute-start | bytes 196616 | tf_op jit(solution)/shard_map/ppermute | solution.py:25
  13.0 6.3 %collective-permute-start.1 = (bf16[1,32,1,1024]{3,2,1,0:T(2,128)(2,1)S(1)}, bf16[1,32,1,1024]{3,2,1,0:T(2,128)(2,1)S(1)}, u32[]{:S(2)}, u32[]{:S(2)}) collective-permute-start(bf16[1,32,1,1024]{3,2,1,0:T(2,128)(2,1)S(1)} %get-tuple-element.87), channel_id=1, source_target_pairs={{1,0},{2,1},{3,2},{4,3},{5,4},{6,5},{7,6},{8,7},{9,8},{10,9},{11,1... | collective-permute-start | bytes 196616 | tf_op jit(solution)/shard_map/ppermute | solution.py:26
  16.0 26.1 %collective-permute-start.10 = (bf16[2,1,1,128,2,64]{3,5,4,0,2,1:T(8,128)(2,1)S(1)}, bf16[2,1,1,128,2,64]{3,5,4,0,2,1:T(8,128)(2,1)S(1)}, u32[]{:S(2)}, u32[]{:S(2)}) collective-permute-start(bf16[2,1,1,128,2,64]{3,5,4,0,2,1:T(8,128)(2,1)S(1)} %select_bitcast_fusion.1), channel_id=1, source_target_pairs={{0,1},{1,0},{2,3},{3,2},{4,5},{5,4},{6,7},{7,6},{8,9},{9,8},{10,11... | collective-permute-start | bytes 196616 | tf_op jit(solution)/shard_map/ppermute | solution.py:38
  17.2 12.9 %copy-start.4 = (bf16[64,864]{0,1:T(8,128)(2,1)}, bf16[64,864]{0,1:T(8,128)(2,1)S(1)}, u32[]{:S(2)}) copy-start(bf16[64,864]{0,1:T(8,128)(2,1)S(1)} %copy.304) | copy-start | bytes 331780
  24.3 5.9 %copy-start.7 = (f32[64]{0:T(128)S(1)}, f32[64]{0:T(128)}, u32[]{:S(2)}) copy-start(f32[64]{0:T(128)} %param.8) | copy-start | bytes 772
  24.3 5.9 %copy-start.9 = (pred[8,3]{0,1:T(4,128)(4,1)S(1)}, pred[8,3]{0,1:T(4,128)(4,1)}, u32[]{:S(2)}) copy-start(pred[8,3]{0,1:T(4,128)(4,1)} %constant.61) | copy-start | bytes 76
  28.2 2.1 copy-start.1
  42.0 1.3 collective-permute-start.2
  43.5 7.1 %collective-permute-start.3 = (bf16[1,2,1,64,2,64]{5,3,4,1,2,0:T(8,128)(2,1)S(1)}, bf16[1,2,1,64,2,64]{5,3,4,1,2,0:T(8,128)(2,1)S(1)}, u32[]{:S(2)}, u32[]{:S(2)}) collective-permute-start(bf16[1,2,1,64,2,64]{5,3,4,1,2,0:T(8,128)(2,1)S(1)} %fusion.222), channel_id=1, source_target_pairs={{0,2},{2,0},{1,3},{3,1},{4,6},{6,4},{5,7},{7,5},{8,10},{10,8},{9,1... | collective-permute-start | bytes 98312 | tf_op jit(solution)/shard_map/ppermute | solution.py:38
  44.8 11.7 %collective-permute-start.11 = (bf16[1,2,1,128,2,64]{3,5,4,1,2,0:T(8,128)(2,1)S(1)}, bf16[1,2,1,128,2,64]{3,5,4,1,2,0:T(8,128)(2,1)S(1)}, u32[]{:S(2)}, u32[]{:S(2)}) collective-permute-start(bf16[1,2,1,128,2,64]{3,5,4,1,2,0:T(8,128)(2,1)S(1)} %select_bitcast_fusion), channel_id=1, source_target_pairs={{0,2},{2,0},{1,3},{3,1},{4,6},{6,4},{5,7},{7,5},{8,10},{10,8},{9,1... | collective-permute-start | bytes 196616 | tf_op jit(solution)/shard_map/ppermute | solution.py:38
  49.1 18.8 %copy-start.8 = (f32[128]{0:T(128)S(1)}, f32[128]{0:T(128)}, u32[]{:S(2)}) copy-start(f32[128]{0:T(128)} %param.10) | copy-start | bytes 1540
  50.8 6.8 %collective-permute-start.5 = (bf16[1,64,64]{1,2,0:T(8,128)(2,1)S(1)}, bf16[1,64,64]{1,2,0:T(8,128)(2,1)S(1)}, u32[]{:S(2)}, u32[]{:S(2)}) collective-permute-start(bf16[1,64,64]{1,2,0:T(8,128)(2,1)S(1)} %get-tuple-element.102), channel_id=1, source_target_pairs={{1,0},{2,1},{3,2},{4,3},{5,4},{6,5},{7,6},{8,7},{9,8},{10,9},{11,1... | collective-permute-start | bytes 24584 | tf_op jit(solution)/shard_map/ppermute | solution.py:44
  53.4 3.9 collective-permute-start.4
  57.8 8.5 %collective-permute-start.7 = (bf16[1,64,80]{1,2,0:T(8,128)(2,1)S(1)}, bf16[1,64,80]{1,2,0:T(8,128)(2,1)S(1)}, u32[]{:S(2)}, u32[]{:S(2)}) collective-permute-start(bf16[1,64,80]{1,2,0:T(8,128)(2,1)S(1)} %bitcast.916), channel_id=1, source_target_pairs={{4,0},{5,1},{6,2},{7,3},{8,4},{9,5},{10,6},{11,7},{12,8},{13,9},{1... | collective-permute-start | bytes 30728 | tf_op jit(solution)/shard_map/ppermute | solution.py:44
  59.1 8.0 %collective-permute-start.6 = (bf16[1,64,80]{1,2,0:T(8,128)(2,1)S(1)}, bf16[1,64,80]{1,2,0:T(8,128)(2,1)S(1)}, u32[]{:S(2)}, u32[]{:S(2)}) collective-permute-start(bf16[1,64,80]{1,2,0:T(8,128)(2,1)S(1)} %bitcast.912), channel_id=1, source_target_pairs={{0,4},{1,5},{2,6},{3,7},{4,8},{5,9},{6,10},{7,11},{8,12},{9,13},{1... | collective-permute-start | bytes 30728 | tf_op jit(solution)/shard_map/ppermute | solution.py:44
  79.2 12.6 %collective-permute-start.13 = (bf16[1,128,64]{1,2,0:T(8,128)(2,1)S(1)}, bf16[1,128,64]{1,2,0:T(8,128)(2,1)S(1)}, u32[]{:S(2)}, u32[]{:S(2)}) collective-permute-start(bf16[1,128,64]{1,2,0:T(8,128)(2,1)S(1)} %bitcast.922), channel_id=1, source_target_pairs={{1,0},{2,1},{3,2},{4,3},{5,4},{6,5},{7,6},{8,7},{9,8},{10,9},{11,1... | collective-permute-start | bytes 49160 | tf_op jit(solution)/shard_map/ppermute | solution.py:44
  82.7 9.2 %collective-permute-start.12 = (bf16[1,128,64]{1,2,0:T(8,128)(2,1)S(1)}, bf16[1,128,64]{1,2,0:T(8,128)(2,1)S(1)}, u32[]{:S(2)}, u32[]{:S(2)}) collective-permute-start(bf16[1,128,64]{1,2,0:T(8,128)(2,1)S(1)} %bitcast.920), channel_id=1, source_target_pairs={{0,1},{1,2},{2,3},{3,4},{4,5},{5,6},{6,7},{7,8},{8,9},{9,10},{10,1... | collective-permute-start | bytes 49160 | tf_op jit(solution)/shard_map/ppermute | solution.py:44
  85.9 20.6 %collective-permute-start.8 = (bf16[2,1,1,128,2,64]{3,5,4,0,2,1:T(8,128)(2,1)S(1)}, bf16[2,1,1,128,2,64]{3,5,4,0,2,1:T(8,128)(2,1)S(1)}, u32[]{:S(2)}, u32[]{:S(2)}) collective-permute-start(bf16[2,1,1,128,2,64]{3,5,4,0,2,1:T(8,128)(2,1)S(1)} %fusion.221), channel_id=1, source_target_pairs={{0,1},{1,0},{2,3},{3,2},{4,5},{5,4},{6,7},{7,6},{8,9},{9,8},{10,11... | collective-permute-start | bytes 196616 | tf_op jit(solution)/shard_map/ppermute | solution.py:38
  92.1 10.6 %collective-permute-start.15 = (bf16[1,128,80]{1,2,0:T(8,128)(2,1)S(1)}, bf16[1,128,80]{1,2,0:T(8,128)(2,1)S(1)}, u32[]{:S(2)}, u32[]{:S(2)}) collective-permute-start(bf16[1,128,80]{1,2,0:T(8,128)(2,1)S(1)} %bitcast.918), channel_id=1, source_target_pairs={{4,0},{5,1},{6,2},{7,3},{8,4},{9,5},{10,6},{11,7},{12,8},{13,9},{1... | collective-permute-start | bytes 61448 | tf_op jit(solution)/shard_map/ppermute | solution.py:44
  93.4 9.4 %collective-permute-start.14 = (bf16[1,128,80]{1,2,0:T(8,128)(2,1)S(1)}, bf16[1,128,80]{1,2,0:T(8,128)(2,1)S(1)}, u32[]{:S(2)}, u32[]{:S(2)}) collective-permute-start(bf16[1,128,80]{1,2,0:T(8,128)(2,1)S(1)} %bitcast.913), channel_id=1, source_target_pairs={{0,4},{1,5},{2,6},{3,7},{4,8},{5,9},{6,10},{7,11},{8,12},{9,13},{1... | collective-permute-start | bytes 61448 | tf_op jit(solution)/shard_map/ppermute | solution.py:44
  101.8 0.9 copy-start.3
  105.9 1.6 collective-permute-start.16
  107.5 6.8 %collective-permute-start.17 = (bf16[1,2,1,64,2,64]{5,3,4,1,2,0:T(8,128)(2,1)S(1)}, bf16[1,2,1,64,2,64]{5,3,4,1,2,0:T(8,128)(2,1)S(1)}, u32[]{:S(2)}, u32[]{:S(2)}) collective-permute-start(bf16[1,2,1,64,2,64]{5,3,4,1,2,0:T(8,128)(2,1)S(1)} %fusion.219), channel_id=1, source_target_pairs={{0,2},{2,0},{1,3},{3,1},{4,6},{6,4},{5,7},{7,5},{8,10},{10,8},{9,1... | collective-permute-start | bytes 98312 | tf_op jit(solution)/shard_map/ppermute | solution.py:38
  112.8 125.9 %collective-permute-start.9 = (bf16[1,2,1,128,2,64]{3,5,4,1,2,0:T(8,128)(2,1)}, bf16[1,2,1,128,2,64]{3,5,4,1,2,0:T(8,128)(2,1)S(1)}, u32[]{:S(2)}, u32[]{:S(2)}) collective-permute-start(bf16[1,2,1,128,2,64]{3,5,4,1,2,0:T(8,128)(2,1)} %fusion.220), channel_id=1, source_target_pairs={{0,2},{2,0},{1,3},{3,1},{4,6},{6,4},{5,7},{7,5},{8,10},{10,8},{9,1... | collective-permute-start | bytes 196616 | tf_op jit(solution)/shard_map/ppermute | solution.py:38
  204.0 35.6 %collective-permute-start.18 = (bf16[1,64,1,1024]{1,3,2,0:T(8,128)(2,1)}, bf16[1,64,1,1024]{1,3,2,0:T(8,128)(2,1)}, u32[]{:S(2)}, u32[]{:S(2)}) collective-permute-start(bf16[1,64,1,1024]{1,3,2,0:T(8,128)(2,1)} %get-tuple-element.47), channel_id=1, source_target_pairs={{0,1},{1,2},{2,3},{3,4},{4,5},{5,6},{6,7},{7,8},{8,9},{9,10},{10,1... | collective-permute-start | bytes 393224 | tf_op jit(solution)/shard_map/ppermute | solution.py:25
  206.8 32.7 %collective-permute-start.19 = (bf16[1,64,1,1024]{1,3,2,0:T(8,128)(2,1)}, bf16[1,64,1,1024]{1,3,2,0:T(8,128)(2,1)}, u32[]{:S(2)}, u32[]{:S(2)}) collective-permute-start(bf16[1,64,1,1024]{1,3,2,0:T(8,128)(2,1)} %get-tuple-element.48), channel_id=1, source_target_pairs={{1,0},{2,1},{3,2},{4,3},{5,4},{6,5},{7,6},{8,7},{9,8},{10,9},{11,1... | collective-permute-start | bytes 393224 | tf_op jit(solution)/shard_map/ppermute | solution.py:26
  247.4 4.8 copy-start.5
  250.3 2.2 copy-start.2
  252.4 12.2 %copy-start.6 = (pred[8,3]{1,0:T(8,128)(4,1)S(1)}, pred[8,3]{1,0:T(8,128)(4,1)}, u32[]{:S(2)}) copy-start(pred[8,3]{1,0:T(8,128)(4,1)} %constant.59) | copy-start | bytes 76
Sparse Core Ops, SparseCore 0:
  238.8 257.5 all-reduce.5
where the time goes:
time: 516 us; the launch traced here: 507 us
  waiting for transfers between devices  237 us (46%)
  blocking collectives  83.8 us (16%)
  matrix products  57.1 us (11%)
  starting transfers between devices  49.4 us (10%)
  local copies, waits for them, and re-layouts  45.7 us (9%)
  other arithmetic  19.6 us (4%)
  between operations  15.1 us (3%)
    psum x1, waiting for transfers between devices, per_device(): lax.psum((first_wgrad, first_bgrad, second_wgrad, second_bgrad), ('sample...  229 us
    psum x1, blocking collectives, per_device(): lax.psum((first_wgrad, first_bgrad, second_wgrad, second_bgrad), ('sample...  83.8 us
    dot_general x54, matrix products, weight_grad(): lax.dot_general(slope_grad, window, (((0, 2, 3, 4), (0, 2, 3, 4)), ((), (...  34 us
    ppermute x8, starting transfers between devices, shifted(): return lax.ppermute(x, axis, pairs)  29.9 us
    conv_general_dilated x4, matrix products, correlate(): lax.conv_general_dilated(padded, kernel, (1, 1, 1), 'VALID', dimension_nu...  23.1 us
    conv_general_dilated x5, local copies, waits for them, and re-layouts, correlate(): lax.conv_general_dilated(padded, kernel, (1, 1, 1), 'VALID', dimension_nu...  11.7 us
    unnamed x37, local copies, waits for them, and re-layouts  11.2 us
  transfers between devices with their start and end apart: 21, of which 7 were waited for; matrix products, arithmetic and copies ran while one was open for 20% of the time, Pallas kernels for 0%

commit v1 on v0

--- a/solution.py
+++ b/solution.py
@@ -183,6 +183,36 @@
     return jnp.pad(full_block, ((0, 0), (0, 0), (0, 0), (0, 0), (1, 1)))
 
 
+def all_summed(parts, axes):
+    flat = jnp.concatenate([part.reshape(-1) for part in parts])
+    levels = []
+    for axis in axes:
+        for bit in range(lax.axis_size(axis).bit_length() - 1):
+            levels.append((axis, bit))
+    block = 1 << len(levels)
+    total = flat.shape[0]
+    current = jnp.pad(flat, (0, -total % block))
+    for axis, bit in levels:
+        half = current.shape[0] // 2
+        upper = (lax.axis_index(axis) >> bit & 1) == 1
+        kept = jnp.where(upper, current[half:], current[:half])
+        sent = jnp.where(upper, current[:half], current[half:])
+        pairs = [(i, i ^ 1 << bit) for i in range(lax.axis_size(axis))]
+        current = kept + lax.ppermute(sent, axis, pairs)
+    for axis, bit in reversed(levels):
+        upper = (lax.axis_index(axis) >> bit & 1) == 1
+        pairs = [(i, i ^ 1 << bit) for i in range(lax.axis_size(axis))]
+        other = lax.ppermute(current, axis, pairs)
+        current = jnp.where(
+            upper, jnp.concatenate([other, current]), jnp.concatenate([current, other])
+        )
+    results, start = [], 0
+    for part in parts:
+        results.append(current[start : start + part.size].reshape(part.shape))
+        start += part.size
+    return tuple(results)
+
+
 def per_device(volumes, first_weight, first_bias, second_weight, second_bias, cotangent):
     sample_count = volumes.shape[0]
     depth_cells = volumes.shape[2]
@@ -265,8 +295,8 @@
     first_grad = upsampled(pooled_cells, silu_slope(first_pre)).astype(jnp.bfloat16)
     first_wgrad = weight_grad(padded_in, first_grad)
     first_bgrad = jnp.sum(first_grad, axis=(0, 2, 3, 4), dtype=jnp.float32)
-    first_wgrad, first_bgrad, second_wgrad, second_bgrad = lax.psum(
-        (first_wgrad, first_bgrad, second_wgrad, second_bgrad), ("sample", "space")
+    first_wgrad, first_bgrad, second_wgrad, second_bgrad = all_summed(
+        (first_wgrad, first_bgrad, second_wgrad, second_bgrad), ("space", "sample")
     )
     flip_one = flipped(kernel_one)
     haloed_grad = padded_2(

time: 516 us -> 281 us (0.54)
  waiting for transfers between devices: 237 us -> 35.9 us
  blocking collectives: 83.8 us -> 0 us
  starting transfers between devices: 49.4 us -> 111 us
  local copies, waits for them, and re-layouts: 45.7 us -> 66.5 us
  matrix products: 57.1 us -> 41.7 us
  between operations: 15.1 us -> 1.85 us
    psum x1 -> x0, waiting for transfers between devices: 229 us -> none  [per_device(): lax.psum((first_wgrad, first_bgrad, second_wgrad, second_bgrad), ('sample...]
    psum x1 -> x0, blocking collectives: 83.8 us -> none  [per_device(): lax.psum((first_wgrad, first_bgrad, second_wgrad, second_bgrad), ('sample...]
    ppermute x0 -> x16, starting transfers between devices: none -> 38.4 us  [the longest x8 24.5 us: all_summed(): current = kept + lax.ppermute(sent, axis, pairs)]
    ppermute x0 -> x16, waiting for transfers between devices: none -> 23.6 us  [the longest x8 17.5 us: all_summed(): current = kept + lax.ppermute(sent, axis, pairs)]
    concatenate x0 -> x4, local copies, waits for them, and re-layouts: none -> 19.7 us  [the longest x2 19.2 us: all_summed(): flat = jnp.concatenate([part.reshape(-1) for part in parts])]
    ppermute x8, starting transfers between devices: 7.65 us -> 27 us  [from_partner(): return lax.ppermute(block, axis, route)]
    dot_general x54, matrix products: 34 us -> 17.8 us  [weight_grad(): lax.dot_general(slope_grad, window, (((0, 2, 3, 4), (0, 2, 3, 4)), ((), (...]
    ppermute x2, waiting for transfers between devices: 2.07 us -> 7.8 us  [padded_2(): after = lax.ppermute(initial, axis, down)]
  transfers between devices with their start and end apart: 21 -> 36, of which waited for: 7 -> 20; matrix products, arithmetic and copies ran while one was open for 20% -> 23% of each run, Pallas kernels for 0% -> 0%
where the time goes in v1:
time: 281 us; the launch traced here: 276 us
  starting transfers between devices  111 us (40%)
  local copies, waits for them, and re-layouts  66.5 us (24%)
  matrix products  41.7 us (15%)
  waiting for transfers between devices  35.9 us (13%)
  other arithmetic  19.6 us (7%)
    ppermute x8, starting transfers between devices, shifted(): return lax.ppermute(x, axis, pairs)  29.4 us
    ppermute x8, starting transfers between devices, from_partner(): return lax.ppermute(block, axis, route)  27 us
    ppermute x8, starting transfers between devices, all_summed(): current = kept + lax.ppermute(sent, axis, pairs)  24.5 us
    conv_general_dilated x4, matrix products, correlate(): lax.conv_general_dilated(padded, kernel, (1, 1, 1), 'VALID', dimension_nu...  23.9 us
    concatenate x2, local copies, waits for them, and re-layouts, all_summed(): flat = jnp.concatenate([part.reshape(-1) for part in parts])  19.2 us
    dot_general x54, matrix products, weight_grad(): lax.dot_general(slope_grad, window, (((0, 2, 3, 4), (0, 2, 3, 4)), ((), (...  17.8 us
    ppermute x8, waiting for transfers between devices, all_summed(): current = kept + lax.ppermute(sent, axis, pairs)  17.5 us
    ppermute x8, starting transfers between devices, all_summed(): other = lax.ppermute(current, axis, pairs)  14 us
  transfers between devices with their start and end apart: 36, of which 20 were waited for; matrix products, arithmetic and copies ran while one was open for 23% of the time, Pallas kernels for 0%

profile of v1, /device:TPU:1, one launch (start us, length us, event | category | flops | bytes accessed | tf_op | source)
XLA Modules:
  0.0 276.1 jit_solution(13580380050083564521)
XLA Ops:
  2.0 4.5 %collective-permute-start = (bf16[1,32,1,1024]{3,2,1,0:T(2,128)(2,1)S(1)}, bf16[1,32,1,1024]{3,2,1,0:T(2,128)(2,1)S(1)}, u32[]{:S(2)}, u32[]{:S(2)}) collective-permute-start(bf16[1,32,1,1024]{3,2,1,0:T(2,128)(2,1)S(1)} %get-tuple-element.76), channel_id=1, source_target_pairs={{0,1},{1,2},{2,3},{3,4},{4,5},{5,6},{6,7},{7,8},{8,9},{9,10},{10,1... | collective-permute-start | bytes 196616 | tf_op jit(solution)/shard_map/ppermute | solution.py:25
  6.5 1.9 collective-permute-start.1
  9.6 1.7 copy.309
  15.0 2.0 copy.492
  18.4 2.6 copy.308
  21.1 2.0 slice.451
  23.2 6.5 %add_multiply_fusion = (f32[4,64,8,3,64]{4,2,3,1,0:T(8,128)}, f32[4,64,8,3,64]{4,2,3,1,0:T(8,128)S(1)}) fusion(f32[64]{0:T(128)S(1)} %copy-done.11, pred[8,3]{0,1:T(4,128)(4,1)S(1)} %copy-done.13, bf16[64,3,3,3,32]{0,4,3,2,1:T(8,128)(2,1)S(1)} %bitcast.908, bf16[32,6,64,1,7,2]{0,4,5,2,1,3:T(8,128)(2,1)S(1)} %slice.451, ...), kind=kOutput, calls=%fused_computation.16 | convolution fusion | flops 679280640 | bytes 4190488 | tf_op jit(solution)/shard_map/conv_general_dilated | solution.py:64
  31.8 2.9 %reduce_sum.27 = f32[64,2,32,8]{0,2,3,1:T(8,128)S(1)} reduce(f32[64,2,2,32,2,8,2]{0,4,3,6,5,2,1:T(2,128)} %bitcast.881, f32[]{:T(128)} %constant.46.clone.1), dimensions={2,4,6}, to_apply=%region_0.1 | reduce | flops 229376 | bytes 1179652 | tf_op jit(solution)/shard_map/reduce_sum | solution.py:238
  39.6 2.4 copy.349
  43.8 2.6 collective-permute-start.5
  46.4 3.0 %collective-permute-start.4 = (bf16[1,64,64]{1,2,0:T(8,128)(2,1)S(1)}, bf16[1,64,64]{1,2,0:T(8,128)(2,1)S(1)}, u32[]{:S(2)}, u32[]{:S(2)}) collective-permute-start(bf16[1,64,64]{1,2,0:T(8,128)(2,1)S(1)} %get-tuple-element.93), channel_id=1, source_target_pairs={{0,1},{1,2},{2,3},{3,4},{4,5},{5,6},{6,7},{7,8},{8,9},{9,10},{10,1... | collective-permute-start | bytes 24584 | tf_op jit(solution)/shard_map/ppermute | solution.py:44
  52.0 7.1 %collective-permute-start.6 = (bf16[1,64,80]{1,2,0:T(8,128)(2,1)S(1)}, bf16[1,64,80]{1,2,0:T(8,128)(2,1)S(1)}, u32[]{:S(2)}, u32[]{:S(2)}) collective-permute-start(bf16[1,64,80]{1,2,0:T(8,128)(2,1)S(1)} %bitcast.914), channel_id=1, source_target_pairs={{0,4},{1,5},{2,6},{3,7},{4,8},{5,9},{6,10},{7,11},{8,12},{9,13},{1... | collective-permute-start | bytes 30728 | tf_op jit(solution)/shard_map/ppermute | solution.py:44
  60.8 3.4 %convert_reduce_fusion.1 = (f32[128]{0:T(128)S(1)}, bf16[1,128,8,8,8]{1,0,4,3,2:T(2,128)(2,1)S(1)}, f32[1,128,8,8,8]{1,0,4,3,2:T(1,128)}, f32[1,128,8,8,8]{1,0,4,3,2:T(1,128)}) fusion(f32[1,128,8,8,8]{1,0,4,3,2:T(1,128)S(1)} %bitcast.906, f32[128]{0:T(128)S(1)} %copy-done.12, bf16[1,64,10,10,8]{1,0,4,3,2:T(2,128)(2,1)S(1)} %pad_maximum_fusion.1, ...), kind=kOutput, calls=%fused_computation.214 | convolution fusion | flops 208404352 | bytes 1463296 | tf_op jit(solution)/shard_map/conv_general_dilated | solution.py:64
  64.3 2.8 %pad_maximum_fusion.4 = (bf16[1,64,8,8,8]{1,0,4,3,2:T(2,128)(2,1)S(1)}, bf16[1,64,8,8,8]{1,0,4,3,2:T(2,128)(2,1)S(1)}, bf16[1,64,8,8,8]{1,0,4,3,2:T(2,128)(2,1)S...) fusion(bf16[1,64,1,10,8]{1,0,4,3,2:T(2,128)(2,1)S(1)} %copy.326, ...), kind=kLoop, calls=%fused_computation.209 | loop fusion | flops 196608 | bytes 495616 | tf_op jit(solution)/shard_map/concatenate | solution.py:175
  67.2 2.9 %pad_slice_fusion.5 = (bf16[1,64,8,8,8]{1,0,4,3,2:T(2,128)(2,1)S(1)}, bf16[1,64,8,8,8]{1,0,4,3,2:T(2,128)(2,1)S(1)}, bf16[1,64,8,8,8]{1,0,4,3,2:T(2,128)(2,1)S(1...) fusion(bf16[1,64,10,10,8]{1,0,4,3,2:T(2,128)(2,1)S(1)} %pad_max, ...), kind=kLoop, calls=%fused_computation.429 | loop fusion | bytes 692224 | tf_op jit(solution)/shard_map/slice | solution.py:96
  70.1 2.9 %pad_slice_fusion.6 = (bf16[1,64,8,8,8]{1,0,4,3,2:T(2,128)(2,1)S(1)}, bf16[1,64,8,8,8]{1,0,4,3,2:T(2,128)(2,1)S(1)}, bf16[1,64,8,8,8]{1,0,4,3,2:T(2,128)(2,1)S(1...) fusion(bf16[1,64,10,10,8]{1,0,4,3,2:T(2,128)(2,1)S(1)} %pad_max, ...), kind=kLoop, calls=%fused_computation.430 | loop fusion | bytes 692224 | tf_op jit(solution)/shard_map/slice | solution.py:96
  72.9 3.5 %collective-permute-start.13 = (bf16[1,128,64]{1,2,0:T(8,128)(2,1)S(1)}, bf16[1,128,64]{1,2,0:T(8,128)(2,1)S(1)}, u32[]{:S(2)}, u32[]{:S(2)}) collective-permute-start(bf16[1,128,64]{1,2,0:T(8,128)(2,1)S(1)} %bitcast.924), channel_id=1, source_target_pairs={{1,0},{2,1},{3,2},{4,3},{5,4},{6,5},{7,6},{8,7},{9,8},{10,9},{11,1... | collective-permute-start | bytes 49160 | tf_op jit(solution)/shard_map/ppermute | solution.py:44
  76.4 2.9 %collective-permute-start.12 = (bf16[1,128,64]{1,2,0:T(8,128)(2,1)S(1)}, bf16[1,128,64]{1,2,0:T(8,128)(2,1)S(1)}, u32[]{:S(2)}, u32[]{:S(2)}) collective-permute-start(bf16[1,128,64]{1,2,0:T(8,128)(2,1)S(1)} %bitcast.922), channel_id=1, source_target_pairs={{0,1},{1,2},{2,3},{3,4},{4,5},{5,6},{6,7},{7,8},{8,9},{9,10},{10,1... | collective-permute-start | bytes 49160 | tf_op jit(solution)/shard_map/ppermute | solution.py:44
  86.1 7.7 %collective-permute-start.14 = (bf16[1,128,80]{1,2,0:T(8,128)(2,1)S(1)}, bf16[1,128,80]{1,2,0:T(8,128)(2,1)S(1)}, u32[]{:S(2)}, u32[]{:S(2)}) collective-permute-start(bf16[1,128,80]{1,2,0:T(8,128)(2,1)S(1)} %bitcast.915), channel_id=1, source_target_pairs={{0,4},{1,5},{2,6},{3,7},{4,8},{5,9},{6,10},{7,11},{8,12},{9,13},{1... | collective-permute-start | bytes 61448 | tf_op jit(solution)/shard_map/ppermute | solution.py:44
  94.7 2.8 %fusion.123 = f32[1,64,8,8,8]{1,0,4,3,2:T(1,128)S(1)} fusion(bf16[128,3,3,3,64]{0,4,3,2,1:T(8,128)(2,1)S(1)} %bitcast.873, bf16[1,128,1,10,8]{1,0,4,3,2:T(2,128)(2,1)S(1)} %copy.343, bf16[1,128,8,1,8]{1,0,4,3,2:T(2,128)(2,1)S(1)} %copy.341, bf16[1,128,8,8,8]{1,0,4,3,2:T(2,128)(2,1)S(1)} %get-tuple-element.31, bf16[1,128,8,1,8]{1,0,4,3,2:T(2,128)(2,1)S(1)} %copy.340, ...), kind=kOutput, calls=%fused_computation.198 | convolution fusion | flops 208642048 | bytes 778240 | tf_op jit(solution)/shard_map/conv_general_dilated | solution.py:64
  100.1 12.4 %collective-permute-start.17 = (bf16[1,2,1,64,2,64]{5,3,4,1,2,0:T(8,128)(2,1)S(1)}, bf16[1,2,1,64,2,64]{5,3,4,1,2,0:T(8,128)(2,1)S(1)}, u32[]{:S(2)}, u32[]{:S(2)}) collective-permute-start(bf16[1,2,1,64,2,64]{5,3,4,1,2,0:T(8,128)(2,1)S(1)} %fusion.219), channel_id=1, source_target_pairs={{0,2},{2,0},{1,3},{3,1},{4,6},{6,4},{5,7},{7,5},{8,10},{10,8},{9,1... | collective-permute-start | bytes 98312 | tf_op jit(solution)/shard_map/ppermute | solution.py:38
  115.8 3.1 %convert_reduce_fusion = (f32[64]{0:T(128)S(1)}, bf16[1,64,4,64,16]{1,4,3,2,0:T(8,128)(2,1)S(1)}) fusion(f32[1,64,4,64,16]{1,4,3,2,0:T(8,128)S(1)} %bitcast.882, f32[4,64,1,16,64]{4,1,3,0,2:T(8,128)} %slice.475), kind=kLoop, calls=%fused_computation.23 | loop fusion | flops 1048512 | bytes 2621696 | tf_op jit(solution)/shard_map/reduce_sum | solution.py:297
  132.3 10.5 %concatenate.114 = f32[276544]{0:T(1024)} concatenate(f32[55296]{0:T(1024)S(1)} %reshape.880, f32[64]{0:T(128)S(1)} %get-tuple-element.33, f32[221184]{0:T(1024)} %reshape.909), dimensions={0} | concatenate | bytes 2212352 | tf_op jit(solution)/shard_map/concatenate | solution.py:187
  142.9 8.7 %concatenate.113 = f32[276672]{0:T(1024)S(1)} concatenate(f32[55296]{0:T(1024)S(1)} %reshape.880, f32[64]{0:T(128)S(1)} %get-tuple-element.33, f32[221184]{0:T(1024)} %reshape.909, f32[128]{0:T(128)S(1)} %get-tuple-element.30), dimensions={0} | concatenate | bytes 2213376 | tf_op jit(solution)/shard_map/concatenate | solution.py:187
  154.0 1.6 collective-permute-done.20
  157.3 6.4 %collective-permute-done.21 = f32[69184]{0:T(1024)S(1)} collective-permute-done((f32[69184]{0:T(1024)S(1)}, f32[69184]{0:T(1024)S(1)}, u32[]{:S(2)}, u32[]{:S(2)}) %collective-permute-start.21) | collective-permute-done | bytes 276768 | tf_op jit(solution)/shard_map/ppermute | solution.py:201
  164.0 4.5 %collective-permute-start.22 = (f32[34592]{0:T(1024)S(1)}, f32[34592]{0:T(1024)S(1)}, u32[]{:S(2)}, u32[]{:S(2)}) collective-permute-start(f32[34592]{0:T(1024)S(1)} %slice_select_fusion.2), channel_id=1, source_target_pairs={{0,4},{1,5},{2,6},{3,7},{4,0},{5,1},{6,2},{7,3},{8,12},{9,13},{10,... | collective-permute-start | bytes 415112 | tf_op jit(solution)/shard_map/ppermute | solution.py:201
  168.5 2.8 %collective-permute-done.22 = f32[34592]{0:T(1024)S(1)} collective-permute-done((f32[34592]{0:T(1024)S(1)}, f32[34592]{0:T(1024)S(1)}, u32[]{:S(2)}, u32[]{:S(2)}) %collective-permute-start.22) | collective-permute-done | bytes 138400 | tf_op jit(solution)/shard_map/ppermute | solution.py:201
  171.6 3.5 %collective-permute-start.23 = (f32[17296]{0:T(1024)S(1)}, f32[17296]{0:T(1024)S(1)}, u32[]{:S(2)}, u32[]{:S(2)}) collective-permute-start(f32[17296]{0:T(1024)S(1)} %slice_select_fusion.4), channel_id=1, source_target_pairs={{0,8},{1,9},{2,10},{3,11},{4,12},{5,13},{6,14},{7,15},{8,0},{9,1},... | collective-permute-start | bytes 207560 | tf_op jit(solution)/shard_map/ppermute | solution.py:201
  175.1 1.7 collective-permute-done.23
  177.0 1.7 collective-permute-start.24
  180.2 3.0 %collective-permute-start.25 = (f32[4324]{0:T(1024)S(1)}, f32[4324]{0:T(1024)S(1)}, u32[]{:S(2)}, u32[]{:S(2)}) collective-permute-start(f32[4324]{0:T(1024)S(1)} %slice_select_fusion.6), channel_id=1, source_target_pairs={{0,32},{16,48},{32,0},{48,16},{64,96},{80,112},{96,64},{112,80},{1... | collective-permute-start | bytes 51896 | tf_op jit(solution)/shard_map/ppermute | solution.py:201
  184.5 6.2 %collective-permute-start.26 = (f32[2162]{0:T(1024)S(1)}, f32[2162]{0:T(1024)S(1)}, u32[]{:S(2)}, u32[]{:S(2)}) collective-permute-start(f32[2162]{0:T(1024)S(1)} %slice_select_fusion.9), channel_id=1, source_target_pairs={{0,64},{16,80},{32,96},{48,112},{64,0},{80,16},{96,32},{112,48},{1... | collective-permute-start | bytes 25952 | tf_op jit(solution)/shard_map/ppermute | solution.py:201
  192.0 2.6 collective-permute-start.27
  196.1 2.6 collective-permute-start.28
  200.2 5.4 %collective-permute-start.29 = (f32[2162]{0:T(1024)S(1)}, f32[2162]{0:T(1024)S(1)}, u32[]{:S(2)}, u32[]{:S(2)}) collective-permute-start(f32[2162]{0:T(1024)S(1)} %maximum_select_fusion.7), channel_id=1, source_target_pairs={{0,64},{16,80},{32,96},{48,112},{64,0},{80,16},{96,32},{112,48},{1... | collective-permute-start | bytes 25952 | tf_op jit(solution)/shard_map/ppermute | solution.py:205
  205.6 9.5 %collective-permute-start.8 = (bf16[2,1,1,128,2,64]{3,5,4,0,2,1:T(8,128)(2,1)S(1)}, bf16[2,1,1,128,2,64]{3,5,4,0,2,1:T(8,128)(2,1)S(1)}, u32[]{:S(2)}, u32[]{:S(2)}) collective-permute-start(bf16[2,1,1,128,2,64]{3,5,4,0,2,1:T(8,128)(2,1)S(1)} %fusion.221), channel_id=1, source_target_pairs={{0,1},{1,0},{2,3},{3,2},{4,5},{5,4},{6,7},{7,6},{8,9},{9,8},{10,11... | collective-permute-start | bytes 196616 | tf_op jit(solution)/shard_map/ppermute | solution.py:38
  216.2 2.6 collective-permute-done.30
  219.4 2.3 collective-permute-done.31
  221.8 1.8 collective-permute-start.32
  226.7 7.4 %collective-permute-start.18 = (bf16[1,64,1,1024]{1,3,2,0:T(8,128)(2,1)S(1)}, bf16[1,64,1,1024]{1,3,2,0:T(8,128)(2,1)S(1)}, u32[]{:S(2)}, u32[]{:S(2)}) collective-permute-start(bf16[1,64,1,1024]{1,3,2,0:T(8,128)(2,1)S(1)} %get-tuple-element.37), channel_id=1, source_target_pairs={{0,1},{1,2},{2,3},{3,4},{4,5},{5,6},{6,7},{7,8},{8,9},{9,10},{10,1... | collective-permute-start | bytes 393224 | tf_op jit(solution)/shard_map/ppermute | solution.py:25
  234.1 1.9 collective-permute-start.19
  238.3 6.4 %collective-permute-done.19 = bf16[1,64,1,1024]{1,3,2,0:T(8,128)(2,1)S(1)} collective-permute-done((bf16[1,64,1,1024]{1,3,2,0:T(8,128)(2,1)S(1)}, bf16[1,64,1,1024]{1,3,2,0:T(8,128)(2,1)S(1)}, u32[]{:S(2)}, u32[]{:S(2)}) %collective-permute-start.19) | collective-permute-done | bytes 131104 | tf_op jit(solution)/shard_map/ppermute | solution.py:26
  246.6 2.2 copy.493
  248.9 2.1 pad.21.clone
  250.9 2.7 copy.353
  253.6 2.0 slice.478
  256.0 11.1 %fusion.4 = bf16[4,64,8,3,32]{4,2,3,1,0:T(8,128)(2,1)S(1)} fusion(bf16[64,3,3,3,32]{0,4,3,2,1:T(8,128)(2,1)S(1)} %bitcast.909, bf16[64,6,64,1,7,2]{0,4,5,2,1,3:T(8,128)(2,1)S(1)} %slice.478, bf16[64,6,64,1,8,3]{0,4,5,2,1,3:T(8,128)(2,1)S(1)} %copy-done.2), kind=kOutput, calls=%fused_computation.6 | convolution fusion | flops 678297600 | bytes 2371584 | tf_op jit(solution)/shard_map/conv_general_dilated | solution.py:64
  (236 shorter events, 77.1 us)
Async XLA Ops:
  0.6 60.2 %copy-start = (bf16[128,1728]{0,1:T(8,128)(2,1)S(1)}, bf16[128,1728]{0,1:T(8,128)(2,1)}, u32[]{:S(2)}) copy-start(bf16[128,1728]{0,1:T(8,128)(2,1)} %param.9) | copy-start | bytes 1327108
  2.0 9.4 %collective-permute-start = (bf16[1,32,1,1024]{3,2,1,0:T(2,128)(2,1)S(1)}, bf16[1,32,1,1024]{3,2,1,0:T(2,128)(2,1)S(1)}, u32[]{:S(2)}, u32[]{:S(2)}) collective-permute-start(bf16[1,32,1,1024]{3,2,1,0:T(2,128)(2,1)S(1)} %get-tuple-element.76), channel_id=1, source_target_pairs={{0,1},{1,2},{2,3},{3,4},{4,5},{5,6},{6,7},{7,8},{8,9},{9,10},{10,1... | collective-permute-start | bytes 196616 | tf_op jit(solution)/shard_map/ppermute | solution.py:25
  6.5 6.3 %collective-permute-start.1 = (bf16[1,32,1,1024]{3,2,1,0:T(2,128)(2,1)S(1)}, bf16[1,32,1,1024]{3,2,1,0:T(2,128)(2,1)S(1)}, u32[]{:S(2)}, u32[]{:S(2)}) collective-permute-start(bf16[1,32,1,1024]{3,2,1,0:T(2,128)(2,1)S(1)} %get-tuple-element.77), channel_id=1, source_target_pairs={{1,0},{2,1},{3,2},{4,3},{5,4},{6,5},{7,6},{8,7},{9,8},{10,9},{11,1... | collective-permute-start | bytes 196616 | tf_op jit(solution)/shard_map/ppermute | solution.py:26
  9.5 25.6 %collective-permute-start.10 = (bf16[2,1,1,128,2,64]{3,5,4,0,2,1:T(8,128)(2,1)S(1)}, bf16[2,1,1,128,2,64]{3,5,4,0,2,1:T(8,128)(2,1)S(1)}, u32[]{:S(2)}, u32[]{:S(2)}) collective-permute-start(bf16[2,1,1,128,2,64]{3,5,4,0,2,1:T(8,128)(2,1)S(1)} %select_bitcast_fusion.1), channel_id=1, source_target_pairs={{0,1},{1,0},{2,3},{3,2},{4,5},{5,4},{6,7},{7,6},{8,9},{9,8},{10,11... | collective-permute-start | bytes 196616 | tf_op jit(solution)/shard_map/ppermute | solution.py:38
  21.1 2.1 copy-start.3
  21.1 2.1 copy-start.8
  21.1 2.1 copy-start.11
  21.1 2.1 copy-start.13
  34.9 1.3 collective-permute-start.2
  36.4 7.2 %collective-permute-start.3 = (bf16[1,2,1,64,2,64]{5,3,4,1,2,0:T(8,128)(2,1)S(1)}, bf16[1,2,1,64,2,64]{5,3,4,1,2,0:T(8,128)(2,1)S(1)}, u32[]{:S(2)}, u32[]{:S(2)}) collective-permute-start(bf16[1,2,1,64,2,64]{5,3,4,1,2,0:T(8,128)(2,1)S(1)} %fusion.222), channel_id=1, source_target_pairs={{0,2},{2,0},{1,3},{3,1},{4,6},{6,4},{5,7},{7,5},{8,10},{10,8},{9,1... | collective-permute-start | bytes 98312 | tf_op jit(solution)/shard_map/ppermute | solution.py:38
  37.7 11.8 %collective-permute-start.11 = (bf16[1,2,1,128,2,64]{3,5,4,1,2,0:T(8,128)(2,1)S(1)}, bf16[1,2,1,128,2,64]{3,5,4,1,2,0:T(8,128)(2,1)S(1)}, u32[]{:S(2)}, u32[]{:S(2)}) collective-permute-start(bf16[1,2,1,128,2,64]{3,5,4,1,2,0:T(8,128)(2,1)S(1)} %select_bitcast_fusion), channel_id=1, source_target_pairs={{0,2},{2,0},{1,3},{3,1},{4,6},{6,4},{5,7},{7,5},{8,10},{10,8},{9,1... | collective-permute-start | bytes 196616 | tf_op jit(solution)/shard_map/ppermute | solution.py:38
  43.6 17.3 %copy-start.12 = (f32[128]{0:T(128)S(1)}, f32[128]{0:T(128)}, u32[]{:S(2)}) copy-start(f32[128]{0:T(128)} %param.10) | copy-start | bytes 1540
  43.8 6.8 %collective-permute-start.5 = (bf16[1,64,64]{1,2,0:T(8,128)(2,1)S(1)}, bf16[1,64,64]{1,2,0:T(8,128)(2,1)S(1)}, u32[]{:S(2)}, u32[]{:S(2)}) collective-permute-start(bf16[1,64,64]{1,2,0:T(8,128)(2,1)S(1)} %get-tuple-element.92), channel_id=1, source_target_pairs={{1,0},{2,1},{3,2},{4,3},{5,4},{6,5},{7,6},{8,7},{9,8},{10,9},{11,1... | collective-permute-start | bytes 24584 | tf_op jit(solution)/shard_map/ppermute | solution.py:44
  46.4 3.9 %collective-permute-start.4 = (bf16[1,64,64]{1,2,0:T(8,128)(2,1)S(1)}, bf16[1,64,64]{1,2,0:T(8,128)(2,1)S(1)}, u32[]{:S(2)}, u32[]{:S(2)}) collective-permute-start(bf16[1,64,64]{1,2,0:T(8,128)(2,1)S(1)} %get-tuple-element.93), channel_id=1, source_target_pairs={{0,1},{1,2},{2,3},{3,4},{4,5},{5,6},{6,7},{7,8},{8,9},{9,10},{10,1... | collective-permute-start | bytes 24584 | tf_op jit(solution)/shard_map/ppermute | solution.py:44
  50.7 8.5 %collective-permute-start.7 = (bf16[1,64,80]{1,2,0:T(8,128)(2,1)S(1)}, bf16[1,64,80]{1,2,0:T(8,128)(2,1)S(1)}, u32[]{:S(2)}, u32[]{:S(2)}) collective-permute-start(bf16[1,64,80]{1,2,0:T(8,128)(2,1)S(1)} %bitcast.917), channel_id=1, source_target_pairs={{4,0},{5,1},{6,2},{7,3},{8,4},{9,5},{10,6},{11,7},{12,8},{13,9},{1... | collective-permute-start | bytes 30728 | tf_op jit(solution)/shard_map/ppermute | solution.py:44
  52.0 8.0 %collective-permute-start.6 = (bf16[1,64,80]{1,2,0:T(8,128)(2,1)S(1)}, bf16[1,64,80]{1,2,0:T(8,128)(2,1)S(1)}, u32[]{:S(2)}, u32[]{:S(2)}) collective-permute-start(bf16[1,64,80]{1,2,0:T(8,128)(2,1)S(1)} %bitcast.914), channel_id=1, source_target_pairs={{0,4},{1,5},{2,6},{3,7},{4,8},{5,9},{6,10},{7,11},{8,12},{9,13},{1... | collective-permute-start | bytes 30728 | tf_op jit(solution)/shard_map/ppermute | solution.py:44
  72.9 11.6 %collective-permute-start.13 = (bf16[1,128,64]{1,2,0:T(8,128)(2,1)S(1)}, bf16[1,128,64]{1,2,0:T(8,128)(2,1)S(1)}, u32[]{:S(2)}, u32[]{:S(2)}) collective-permute-start(bf16[1,128,64]{1,2,0:T(8,128)(2,1)S(1)} %bitcast.924), channel_id=1, source_target_pairs={{1,0},{2,1},{3,2},{4,3},{5,4},{6,5},{7,6},{8,7},{9,8},{10,9},{11,1... | collective-permute-start | bytes 49160 | tf_op jit(solution)/shard_map/ppermute | solution.py:44
  76.4 8.2 %collective-permute-start.12 = (bf16[1,128,64]{1,2,0:T(8,128)(2,1)S(1)}, bf16[1,128,64]{1,2,0:T(8,128)(2,1)S(1)}, u32[]{:S(2)}, u32[]{:S(2)}) collective-permute-start(bf16[1,128,64]{1,2,0:T(8,128)(2,1)S(1)} %bitcast.922), channel_id=1, source_target_pairs={{0,1},{1,2},{2,3},{3,4},{4,5},{5,6},{6,7},{7,8},{8,9},{9,10},{10,1... | collective-permute-start | bytes 49160 | tf_op jit(solution)/shard_map/ppermute | solution.py:44
  84.8 9.2 %collective-permute-start.15 = (bf16[1,128,80]{1,2,0:T(8,128)(2,1)S(1)}, bf16[1,128,80]{1,2,0:T(8,128)(2,1)S(1)}, u32[]{:S(2)}, u32[]{:S(2)}) collective-permute-start(bf16[1,128,80]{1,2,0:T(8,128)(2,1)S(1)} %bitcast.920), channel_id=1, source_target_pairs={{4,0},{5,1},{6,2},{7,3},{8,4},{9,5},{10,6},{11,7},{12,8},{13,9},{1... | collective-permute-start | bytes 61448 | tf_op jit(solution)/shard_map/ppermute | solution.py:44
  86.1 8.6 %collective-permute-start.14 = (bf16[1,128,80]{1,2,0:T(8,128)(2,1)S(1)}, bf16[1,128,80]{1,2,0:T(8,128)(2,1)S(1)}, u32[]{:S(2)}, u32[]{:S(2)}) collective-permute-start(bf16[1,128,80]{1,2,0:T(8,128)(2,1)S(1)} %bitcast.915), channel_id=1, source_target_pairs={{0,4},{1,5},{2,6},{3,7},{4,8},{5,9},{6,10},{7,11},{8,12},{9,13},{1... | collective-permute-start | bytes 61448 | tf_op jit(solution)/shard_map/ppermute | solution.py:44
  97.7 2.3 collective-permute-start.16
  100.1 14.7 %collective-permute-start.17 = (bf16[1,2,1,64,2,64]{5,3,4,1,2,0:T(8,128)(2,1)S(1)}, bf16[1,2,1,64,2,64]{5,3,4,1,2,0:T(8,128)(2,1)S(1)}, u32[]{:S(2)}, u32[]{:S(2)}) collective-permute-start(bf16[1,2,1,64,2,64]{5,3,4,1,2,0:T(8,128)(2,1)S(1)} %fusion.219), channel_id=1, source_target_pairs={{0,2},{2,0},{1,3},{3,1},{4,6},{6,4},{5,7},{7,5},{8,10},{10,8},{9,1... | collective-permute-start | bytes 98312 | tf_op jit(solution)/shard_map/ppermute | solution.py:38
  151.5 4.0 %copy-start.4 = (f32[276544]{0:T(1024)S(1)}, f32[276544]{0:T(1024)}, u32[]{:S(2)}) copy-start(f32[276544]{0:T(1024)} %concatenate.114) | copy-start | bytes 3318532
  152.7 2.8 %collective-permute-start.20 = (f32[138368]{0:T(1024)S(1)}, f32[138368]{0:T(1024)S(1)}, u32[]{:S(2)}, u32[]{:S(2)}) collective-permute-start(f32[138368]{0:T(1024)S(1)} %slice_select_fusion), channel_id=1, source_target_pairs={{0,1},{1,0},{2,3},{3,2},{4,5},{5,4},{6,7},{7,6},{8,9},{9,8},{10,11... | collective-permute-start | bytes 1660424 | tf_op jit(solution)/shard_map/ppermute | solution.py:201
  155.6 43.1 %copy-start.5 = (f32[1,128,8,8,8]{1,0,4,3,2:T(1,128)S(1)}, f32[1,128,8,8,8]{1,0,4,3,2:T(1,128)}, u32[]{:S(2)}) copy-start(f32[1,128,8,8,8]{1,0,4,3,2:T(1,128)} %get-tuple-element.32) | copy-start | bytes 786436
  155.6 43.1 %copy-start.6 = (f32[1,128,8,8,8]{1,0,4,3,2:T(1,128)S(1)}, f32[1,128,8,8,8]{1,0,4,3,2:T(1,128)}, u32[]{:S(2)}) copy-start(f32[1,128,8,8,8]{1,0,4,3,2:T(1,128)} %get-tuple-element.94) | copy-start | bytes 786436
  155.8 7.9 %collective-permute-start.21 = (f32[69184]{0:T(1024)S(1)}, f32[69184]{0:T(1024)S(1)}, u32[]{:S(2)}, u32[]{:S(2)}) collective-permute-start(f32[69184]{0:T(1024)S(1)} %slice_select_fusion.1), channel_id=1, source_target_pairs={{0,2},{1,3},{2,0},{3,1},{4,6},{5,7},{6,4},{7,5},{8,10},{9,11},{10,... | collective-permute-start | bytes 830216 | tf_op jit(solution)/shard_map/ppermute | solution.py:201
  164.0 7.4 %collective-permute-start.22 = (f32[34592]{0:T(1024)S(1)}, f32[34592]{0:T(1024)S(1)}, u32[]{:S(2)}, u32[]{:S(2)}) collective-permute-start(f32[34592]{0:T(1024)S(1)} %slice_select_fusion.2), channel_id=1, source_target_pairs={{0,4},{1,5},{2,6},{3,7},{4,0},{5,1},{6,2},{7,3},{8,12},{9,13},{10,... | collective-permute-start | bytes 415112 | tf_op jit(solution)/shard_map/ppermute | solution.py:201
  171.6 5.2 %collective-permute-start.23 = (f32[17296]{0:T(1024)S(1)}, f32[17296]{0:T(1024)S(1)}, u32[]{:S(2)}, u32[]{:S(2)}) collective-permute-start(f32[17296]{0:T(1024)S(1)} %slice_select_fusion.4), channel_id=1, source_target_pairs={{0,8},{1,9},{2,10},{3,11},{4,12},{5,13},{6,14},{7,15},{8,0},{9,1},... | collective-permute-start | bytes 207560 | tf_op jit(solution)/shard_map/ppermute | solution.py:201
  177.0 3.1 %collective-permute-start.24 = (f32[8648]{0:T(1024)S(1)}, f32[8648]{0:T(1024)S(1)}, u32[]{:S(2)}, u32[]{:S(2)}) collective-permute-start(f32[8648]{0:T(1024)S(1)} %slice_select_fusion.5), channel_id=1, source_target_pairs={{0,16},{16,0},{32,48},{48,32},{64,80},{80,64},{96,112},{112,96},{1... | collective-permute-start | bytes 103784 | tf_op jit(solution)/shard_map/ppermute | solution.py:201
  180.2 4.2 %collective-permute-start.25 = (f32[4324]{0:T(1024)S(1)}, f32[4324]{0:T(1024)S(1)}, u32[]{:S(2)}, u32[]{:S(2)}) collective-permute-start(f32[4324]{0:T(1024)S(1)} %slice_select_fusion.6), channel_id=1, source_target_pairs={{0,32},{16,48},{32,0},{48,16},{64,96},{80,112},{96,64},{112,80},{1... | collective-permute-start | bytes 51896 | tf_op jit(solution)/shard_map/ppermute | solution.py:201
  184.5 7.3 %collective-permute-start.26 = (f32[2162]{0:T(1024)S(1)}, f32[2162]{0:T(1024)S(1)}, u32[]{:S(2)}, u32[]{:S(2)}) collective-permute-start(f32[2162]{0:T(1024)S(1)} %slice_select_fusion.9), channel_id=1, source_target_pairs={{0,64},{16,80},{32,96},{48,112},{64,0},{80,16},{96,32},{112,48},{1... | collective-permute-start | bytes 25952 | tf_op jit(solution)/shard_map/ppermute | solution.py:201
  192.0 4.0 %collective-permute-start.27 = (f32[1081]{0:T(1024)S(1)}, f32[1081]{0:T(1024)S(1)}, u32[]{:S(2)}, u32[]{:S(2)}) collective-permute-start(f32[1081]{0:T(1024)S(1)} %slice_select_fusion.10), channel_id=1, source_target_pairs={{0,128},{16,144},{32,160},{48,176},{64,192},{80,208},{96,224},{112... | collective-permute-start | bytes 12980 | tf_op jit(solution)/shard_map/ppermute | solution.py:201
  196.1 4.0 %collective-permute-start.28 = (f32[1081]{0:T(1024)S(1)}, f32[1081]{0:T(1024)S(1)}, u32[]{:S(2)}, u32[]{:S(2)}) collective-permute-start(f32[1081]{0:T(1024)S(1)} %select_add_fusion.8), channel_id=1, source_target_pairs={{0,128},{16,144},{32,160},{48,176},{64,192},{80,208},{96,224},{112... | collective-permute-start | bytes 12980 | tf_op jit(solution)/shard_map/ppermute | solution.py:205
  200.2 14.9 %collective-permute-start.29 = (f32[2162]{0:T(1024)S(1)}, f32[2162]{0:T(1024)S(1)}, u32[]{:S(2)}, u32[]{:S(2)}) collective-permute-start(f32[2162]{0:T(1024)S(1)} %maximum_select_fusion.7), channel_id=1, source_target_pairs={{0,64},{16,80},{32,96},{48,112},{64,0},{80,16},{96,32},{112,48},{1... | collective-permute-start | bytes 25952 | tf_op jit(solution)/shard_map/ppermute | solution.py:205
  205.6 10.6 %collective-permute-start.8 = (bf16[2,1,1,128,2,64]{3,5,4,0,2,1:T(8,128)(2,1)S(1)}, bf16[2,1,1,128,2,64]{3,5,4,0,2,1:T(8,128)(2,1)S(1)}, u32[]{:S(2)}, u32[]{:S(2)}) collective-permute-start(bf16[2,1,1,128,2,64]{3,5,4,0,2,1:T(8,128)(2,1)S(1)} %fusion.221), channel_id=1, source_target_pairs={{0,1},{1,0},{2,3},{3,2},{4,5},{5,4},{6,7},{7,6},{8,9},{9,8},{10,11... | collective-permute-start | bytes 196616 | tf_op jit(solution)/shard_map/ppermute | solution.py:38
  215.2 3.6 %collective-permute-start.30 = (f32[4324]{0:T(1024)S(1)}, f32[4324]{0:T(1024)S(1)}, u32[]{:S(2)}, u32[]{:S(2)}) collective-permute-start(f32[4324]{0:T(1024)S(1)} %maximum_select_fusion.6), channel_id=1, source_target_pairs={{0,32},{16,48},{32,0},{48,16},{64,96},{80,112},{96,64},{112,80},{1... | collective-permute-start | bytes 51896 | tf_op jit(solution)/shard_map/ppermute | solution.py:205
  218.8 2.9 %collective-permute-start.31 = (f32[8648]{0:T(1024)S(1)}, f32[8648]{0:T(1024)S(1)}, u32[]{:S(2)}, u32[]{:S(2)}) collective-permute-start(f32[8648]{0:T(1024)S(1)} %maximum_select_fusion.5), channel_id=1, source_target_pairs={{0,16},{16,0},{32,48},{48,32},{64,80},{80,64},{96,112},{112,96},{1... | collective-permute-start | bytes 103784 | tf_op jit(solution)/shard_map/ppermute | solution.py:205
  221.8 3.5 %collective-permute-start.32 = (f32[17296]{0:T(1024)S(1)}, f32[17296]{0:T(1024)S(1)}, u32[]{:S(2)}, u32[]{:S(2)}) collective-permute-start(f32[17296]{0:T(1024)S(1)} %maximum_select_fusion.4), channel_id=1, source_target_pairs={{0,8},{1,9},{2,10},{3,11},{4,12},{5,13},{6,14},{7,15},{8,0},{9,1},... | collective-permute-start | bytes 207560 | tf_op jit(solution)/shard_map/ppermute | solution.py:205
  223.6 13.8 %collective-permute-start.9 = (bf16[1,2,1,128,2,64]{3,5,4,1,2,0:T(8,128)(2,1)S(1)}, bf16[1,2,1,128,2,64]{3,5,4,1,2,0:T(8,128)(2,1)S(1)}, u32[]{:S(2)}, u32[]{:S(2)}) collective-permute-start(bf16[1,2,1,128,2,64]{3,5,4,1,2,0:T(8,128)(2,1)S(1)} %fusion.220), channel_id=1, source_target_pairs={{0,2},{2,0},{1,3},{3,1},{4,6},{6,4},{5,7},{7,5},{8,10},{10,8},{9,1... | collective-permute-start | bytes 196616 | tf_op jit(solution)/shard_map/ppermute | solution.py:38
  225.4 10.6 %collective-permute-start.33 = (f32[34592]{0:T(1024)S(1)}, f32[34592]{0:T(1024)S(1)}, u32[]{:S(2)}, u32[]{:S(2)}) collective-permute-start(f32[34592]{0:T(1024)S(1)} %maximum_select_fusion.3), channel_id=1, source_target_pairs={{0,4},{1,5},{2,6},{3,7},{4,0},{5,1},{6,2},{7,3},{8,12},{9,13},{10,... | collective-permute-start | bytes 415112 | tf_op jit(solution)/shard_map/ppermute | solution.py:205
  226.7 11.5 %collective-permute-start.18 = (bf16[1,64,1,1024]{1,3,2,0:T(8,128)(2,1)S(1)}, bf16[1,64,1,1024]{1,3,2,0:T(8,128)(2,1)S(1)}, u32[]{:S(2)}, u32[]{:S(2)}) collective-permute-start(bf16[1,64,1,1024]{1,3,2,0:T(8,128)(2,1)S(1)} %get-tuple-element.37), channel_id=1, source_target_pairs={{0,1},{1,2},{2,3},{3,4},{4,5},{5,6},{6,7},{7,8},{8,9},{9,10},{10,1... | collective-permute-start | bytes 393224 | tf_op jit(solution)/shard_map/ppermute | solution.py:25
  234.1 10.5 %collective-permute-start.19 = (bf16[1,64,1,1024]{1,3,2,0:T(8,128)(2,1)S(1)}, bf16[1,64,1,1024]{1,3,2,0:T(8,128)(2,1)S(1)}, u32[]{:S(2)}, u32[]{:S(2)}) collective-permute-start(bf16[1,64,1,1024]{1,3,2,0:T(8,128)(2,1)S(1)} %get-tuple-element.38), channel_id=1, source_target_pairs={{1,0},{2,1},{3,2},{4,3},{5,4},{6,5},{7,6},{8,7},{9,8},{10,9},{11,1... | collective-permute-start | bytes 393224 | tf_op jit(solution)/shard_map/ppermute | solution.py:26
  236.2 19.4 %collective-permute-start.34 = (f32[69184]{0:T(1024)S(1)}, f32[69184]{0:T(1024)S(1)}, u32[]{:S(2)}, u32[]{:S(2)}) collective-permute-start(f32[69184]{0:T(1024)S(1)} %maximum_select_fusion.2), channel_id=1, source_target_pairs={{0,2},{1,3},{2,0},{3,1},{4,6},{5,7},{6,4},{7,5},{8,10},{9,11},{10,... | collective-permute-start | bytes 830216 | tf_op jit(solution)/shard_map/ppermute | solution.py:205
  253.6 2.3 copy-start.2
  253.6 2.3 copy-start.9
  255.8 14.8 %collective-permute-start.35 = (f32[138368]{0:T(1024)S(1)}, f32[138368]{0:T(1024)}, u32[]{:S(2)}, u32[]{:S(2)}) collective-permute-start(f32[138368]{0:T(1024)S(1)} %maximum_select_fusion.1), channel_id=1, source_target_pairs={{0,1},{1,0},{2,3},{3,2},{4,5},{5,4},{6,7},{7,6},{8,9},{9,8},{10,11... | collective-permute-start | bytes 1660424 | tf_op jit(solution)/shard_map/ppermute | solution.py:205
  273.1 2.7 copy-start.1
  (2 other events, 1.9 us)
